TPU v7x, 32 devices: a whole 2x2x4 slice. The times are simulated.
32 devices in a mesh: req: 2 (over x), tile: 16 (over z, y, core).
Axes of the slice: x: 2, y: 2, z: 4, core: 2. Of those that a mesh axis runs over, the one named last changes fastest.
Arguments:
- queries: bfloat16 [32, 512, 384], P(('req', 'tile')), parts along dimension 0, may hold values from -12 to 12
- keys: bfloat16 [32, 512, 384], P(('req', 'tile')), parts along dimension 0, may hold values from -5 to 5
- values: bfloat16 [32, 512, 384], P(('req', 'tile')), parts along dimension 0, may hold values from -6 to 6
- text_keys: bfloat16 [512, 1536], P(('req', 'tile')), parts along dimension 0, may hold values from -6 to 6
- text_values: bfloat16 [512, 1536], P(('req', 'tile')), parts along dimension 0, may hold values from -6 to 6
- text_mask: int32 [512], P(('req', 'tile')), parts along dimension 0, may hold values 0 or 1
Outputs:
- attended: bfloat16 [32, 512, 384], P(('req', 'tile')), parts along dimension 0
There are 2 independent parts, one for each index of `req`. A program takes and returns all parts, laid end to end along the dimension named above; each array names one. Nothing has to cross between parts.
All inputs are finite; a program needn't handle non-finite values. No bound on the sum of `text_mask` on one device may be relied on, other than what follows from the above.
Results may differ from a plain program's by a relative error of at most 0.004.
Values may be sent and summed in bfloat16 or wider, within the bound.
No kernel may reach another device: no remote copies, remote signals or barrier semaphores. Data moves between devices by JAX's collectives and lax.ppermute only.
A program may use at most 192 MiB of HBM per device.

v0:
```python
import math
import jax
import jax.numpy as jnp
from jax import lax
from jax.sharding import PartitionSpec as P

TS = 8
HEAD_DIM = 128
HEAD_GROUPS = 4
MASKED = -1e30


def passed_along(value, axis, steps):
    count = lax.axis_size(axis)
    first, last = (max(0, -steps), min(count, count - steps))
    return lax.ppermute(value, axis, [(source, source + steps) for source in range(first, last)])


def shortened(value):
    return jax.tree.map(lambda a: a.astype(jnp.bfloat16) if a.dtype == jnp.float32 else a, value)


def fold_block(running, query_heads, key_block, value_block, key_keep):
    row_top, row_total, summed = running
    head_count = query_heads.shape[1]
    key_heads = key_block.reshape(key_block.shape[0], head_count, HEAD_DIM)
    value_heads = value_block.reshape(value_block.shape[0], head_count, HEAD_DIM)
    scores = jnp.einsum("qhd,khd->hqk", query_heads, key_heads, preferred_element_type=jnp.float32)
    scores = scores * (1.0 / math.sqrt(HEAD_DIM))
    scores = jnp.where(key_keep[None, None, :], scores, MASKED)
    new_top = jnp.maximum(row_top, jnp.max(scores, axis=-1))
    scale_down = jnp.exp(row_top - new_top)
    exp_terms = jnp.where(key_keep[None, None, :], jnp.exp(scores - new_top[:, :, None]), 0.0)
    row_total = row_total * scale_down + jnp.sum(exp_terms, axis=-1)
    weights = exp_terms.astype(jnp.bfloat16)
    summed = summed * scale_down[:, :, None] + jnp.einsum(
        "hqk,khd->hqd", weights, value_heads, preferred_element_type=jnp.float32
    )
    return (new_top, row_total, summed)


def shards(queries, keys, values, text_keys, text_values, text_mask):
    tokens = queries.shape[1]
    lane_width = queries.shape[2]
    head_count = lane_width // HEAD_DIM
    query_heads = queries[0].reshape(tokens, head_count, HEAD_DIM)
    own_pair = jnp.stack([keys[0], values[0]])
    group_count = HEAD_GROUPS
    tiles_all = lax.axis_size("tile") // group_count
    grid_w = min(4, tiles_all)
    grid_h = min(4, tiles_all // grid_w)
    grid_f = tiles_all // (grid_w * grid_h)
    frames_valid = grid_f * TS - TS // 4
    my_index = lax.axis_index("tile")
    tile_id = my_index // group_count
    head_group = my_index % group_count
    w_pos = tile_id % grid_w
    h_pos = tile_id // grid_w % grid_h
    f_pos = tile_id // (grid_w * grid_h)
    local_frame = jnp.arange(tokens, dtype=jnp.int32) // (TS * TS)

    def keep_mask(off_frame, off_height, off_width):
        inside = (
            (f_pos + off_frame >= 0)
            & (f_pos + off_frame < grid_f)
            & (h_pos + off_height >= 0)
            & (h_pos + off_height < grid_h)
            & (w_pos + off_width >= 0)
            & (w_pos + off_width < grid_w)
        )
        return inside & ((f_pos + off_frame) * TS + local_frame < frames_valid)

    running = (
        jnp.full((head_count, tokens), MASKED, jnp.float32),
        jnp.zeros((head_count, tokens), jnp.float32),
        jnp.zeros((head_count, tokens, HEAD_DIM), jnp.float32),
    )
    text_flags = text_mask.astype(jnp.bfloat16)
    piece_keys = lax.dynamic_slice_in_dim(
        lax.all_gather(text_keys, "tile", axis=0, tiled=True),
        head_group * lane_width,
        lane_width,
        1,
    )
    piece_values = lax.dynamic_slice_in_dim(
        lax.all_gather(text_values, "tile", axis=0, tiled=True),
        head_group * lane_width,
        lane_width,
        1,
    )
    running = fold_block(
        running,
        query_heads,
        piece_keys,
        piece_values,
        lax.all_gather(text_flags, "tile", axis=0, tiled=True) > 0.5,
    )
    running = fold_block(running, query_heads, own_pair[0], own_pair[1], keep_mask(0, 0, 0))
    width_set = {0: own_pair}
    for off_width in (-1, 1):
        width_set[off_width] = passed_along(own_pair, "tile", -off_width * group_count)
    width_offsets = sorted(width_set)
    row_stack = jnp.stack([width_set[spot] for spot in width_offsets])
    height_set = {0: row_stack}
    if grid_h > 1:
        for off_height in (-1, 1):
            height_set[off_height] = passed_along(
                shortened(row_stack), "tile", -off_height * grid_w * group_count
            ).astype(row_stack.dtype)
    height_offsets = sorted(height_set)
    slab_stack = jnp.stack([height_set[spot] for spot in height_offsets])

    def fold_slab(state_now, slab_pairs, off_frame):
        for h_slot, off_height in enumerate(height_offsets):
            for w_slot, off_width in enumerate(width_offsets):
                if off_frame == 0 and off_height == 0 and (off_width == 0):
                    continue
                state_now = fold_block(
                    state_now,
                    query_heads,
                    slab_pairs[h_slot, w_slot, 0],
                    slab_pairs[h_slot, w_slot, 1],
                    keep_mask(off_frame, off_height, off_width),
                )
        return state_now

    running = fold_slab(running, slab_stack, 0)
    if grid_f > 1:
        for off_frame in (-1, 1):
            got_slab = passed_along(
                shortened(slab_stack), "tile", -off_frame * grid_h * grid_w * group_count
            ).astype(slab_stack.dtype)
            running = fold_slab(running, got_slab, off_frame)
    row_top, row_total, summed = running
    result = summed / row_total[:, :, None]
    result = jnp.transpose(result, (1, 0, 2)).reshape(tokens, lane_width)
    return result.astype(jnp.bfloat16)[None]


def solution(mesh):
    return jax.shard_map(
        shards,
        mesh=mesh,
        in_specs=(
            P(("req", "tile"), None, None),
            P(("req", "tile"), None, None),
            P(("req", "tile"), None, None),
            P(("req", "tile"), None),
            P(("req", "tile"), None),
            P(("req", "tile")),
        ),
        out_specs=P(("req", "tile"), None, None),
        check_vma=False,
    )
```

profile of v0, /device:TPU:0, one launch (start us, length us, event | category | flops | bytes accessed | tf_op | source)
XLA Modules:
  0.0 110.9 jit_solution(2474602428731131896)
XLA Ops:
  0.0 1.2 %copy.51 = bf16[1,512,384]{1,2,0:T(8,128)(2,1)S(1)} copy(bf16[1,512,384]{2,1,0:T(8,128)(2,1)} %param.7) | data formatting | bytes 786432 | tf_op args[1]
  1.2 1.2 %copy.56 = bf16[1,512,384]{1,2,0:T(8,128)(2,1)S(1)} copy(bf16[1,512,384]{2,1,0:T(8,128)(2,1)} %param.8) | data formatting | bytes 786432 | tf_op args[2]
  2.4 1.0 fusion.71
  3.4 1.3 %collective-permute-start.1 = (bf16[2,512,384]{1,2,0:T(8,128)(2,1)}, bf16[2,512,384]{1,2,0:T(8,128)(2,1)}, u32[]{:S(2)}, u32[]{:S(2)}) collective-permute-start(bf16[2,512,384]{1,2,0:T(8,128)(2,1)} %get-tuple-element.16), channel_id=1, source_target_pairs={{4,0},{5,1},{6,2},{7,3},{8,4},{9,5},{10,6},{11,7},{12,8},{13,9},{1... | collective-permute-start | bytes 2359304 | tf_op jit(solution)/shard_map/ppermute | solution.py:16
  4.7 6.5 %collective-permute-start = (bf16[2,512,384]{1,2,0:T(8,128)(2,1)}, bf16[2,512,384]{1,2,0:T(8,128)(2,1)}, u32[]{:S(2)}, u32[]{:S(2)}) collective-permute-start(bf16[2,512,384]{1,2,0:T(8,128)(2,1)} %get-tuple-element.16), channel_id=1, source_target_pairs={{0,4},{1,5},{2,6},{3,7},{4,8},{5,9},{6,10},{7,11},{8,12},{9,13},{1... | collective-permute-start | bytes 2359304 | tf_op jit(solution)/shard_map/ppermute | solution.py:16
  11.1 0.0 copy-done.2
  11.2 0.6 dynamic-slice
  12.4 0.2 dynamic-update-slice
  12.7 41.9 %all-reduce = bf16[256]{0:T(256)(128)(2,1)S(1)} all-reduce(bf16[256]{0:T(256)(128)(2,1)S(1)} %dynamic-update-slice), channel_id=1, replica_groups=mesh['req'=2,'tile'=16] {'tile'}, use_global_device_ids=true, to_apply=%add | all-reduce | flops 256 | bytes 1024
  54.6 0.2 copy.46
  54.8 19.6 %all_gather.10 = bf16[256,1536]{1,0:T(8,128)(2,1)S(1)} all-gather(bf16[16,1536]{1,0:T(8,128)(2,1)S(1)} %copy-done.1), channel_id=1, replica_groups=mesh['req'=2,'tile'=16] {'tile'}, dimensions={0}, use_global_device_ids=true | all-gather | bytes 835584 | tf_op jit(solution)/shard_map/all_gather | solution.py:80
  74.4 21.4 %all_gather.11 = bf16[256,1536]{1,0:T(8,128)(2,1)S(1)} all-gather(bf16[16,1536]{1,0:T(8,128)(2,1)} %param.10), channel_id=1, replica_groups=mesh['req'=2,'tile'=16] {'tile'}, dimensions={0}, use_global_device_ids=true | all-gather | bytes 835584 | tf_op jit(solution)/shard_map/all_gather | solution.py:86
  95.8 0.8 constant_dynamic-slice_fusion
  96.6 1.1 copy.49
  97.6 1.1 copy.79
  98.8 0.4 bitcast_reduce_fusion.2
  99.2 0.8 fusion.4
  100.0 0.0 collective-permute-done.1
  100.0 0.0 collective-permute-done
  100.0 1.6 %maximum_bitcast_fusion = bf16[1,3,2,512,384]{3,4,2,1,0:T(8,128)(2,1)S(1)} fusion(bf16[1,2,512,384]{2,3,1,0:T(8,128)(2,1)} %bitcast.13, bf16[1,2,512,384]{2,3,1,0:T(8,128)(2,1)S(1)} %get-tuple-element.15, bf16[1,2,512,384]{2,3,1,0:T(8,128)(2,1)} %bitcast.11), kind=kLoop, calls=%fused_computation.13 | loop fusion | flops 2359296 | bytes 4718592 | tf_op jit(solution)/shard_map/stack | solution.py:111
  101.7 0.1 fusion.75
  101.8 0.8 bitcast_reduce_fusion
  102.6 0.8 bitcast_reduce_fusion.1
  103.5 0.9 fusion.9
  104.3 1.0 fusion.38
  105.3 0.9 fusion.7
  106.2 1.0 fusion.35
  107.2 0.9 fusion.5
  108.1 1.0 fusion.24
  109.1 0.3 fusion.41
  109.4 0.6 fusion.43
  110.0 0.9 copy.66
  (14 shorter events, 0.1 us)
Async XLA Ops:
  0.0 11.2 %copy-start.3 = (u32[32]{0:T(128)S(1)}, u32[32]{0:T(128)}, u32[]{:S(2)}) copy-start(u32[32]{0:T(128)} %constant.104) | copy-start | bytes 388
  0.0 11.1 %copy-start.2 = (s32[16]{0:T(128)S(1)}, s32[16]{0:T(128)}, u32[]{:S(2)}) copy-start(s32[16]{0:T(128)} %param.11) | copy-start | bytes 196
  0.0 54.6 %copy-start = (bf16[1,512,384]{2,1,0:T(8,128)(2,1)S(1)}, bf16[1,512,384]{2,1,0:T(8,128)(2,1)}, u32[]{:S(2)}) copy-start(bf16[1,512,384]{2,1,0:T(8,128)(2,1)} %param.6) | copy-start | bytes 1179652
  0.0 54.8 %copy-start.1 = (bf16[16,1536]{1,0:T(8,128)(2,1)S(1)}, bf16[16,1536]{1,0:T(8,128)(2,1)}, u32[]{:S(2)}) copy-start(bf16[16,1536]{1,0:T(8,128)(2,1)} %param.9) | copy-start | bytes 147460
  3.4 96.6 %collective-permute-start.1 = (bf16[2,512,384]{1,2,0:T(8,128)(2,1)}, bf16[2,512,384]{1,2,0:T(8,128)(2,1)}, u32[]{:S(2)}, u32[]{:S(2)}) collective-permute-start(bf16[2,512,384]{1,2,0:T(8,128)(2,1)} %get-tuple-element.16), channel_id=1, source_target_pairs={{4,0},{5,1},{6,2},{7,3},{8,4},{9,5},{10,6},{11,7},{12,8},{13,9},{1... | collective-permute-start | bytes 2359304 | tf_op jit(solution)/shard_map/ppermute | solution.py:16
  4.7 95.4 %collective-permute-start = (bf16[2,512,384]{1,2,0:T(8,128)(2,1)}, bf16[2,512,384]{1,2,0:T(8,128)(2,1)}, u32[]{:S(2)}, u32[]{:S(2)}) collective-permute-start(bf16[2,512,384]{1,2,0:T(8,128)(2,1)} %get-tuple-element.16), channel_id=1, source_target_pairs={{0,4},{1,5},{2,6},{3,7},{4,8},{5,9},{6,10},{7,11},{8,12},{9,13},{1... | collective-permute-start | bytes 2359304 | tf_op jit(solution)/shard_map/ppermute | solution.py:16
where the time goes:
time: 111 us
  blocking collectives  82.9 us (75%)
  starting transfers between devices  7.75 us (7%)
  local copies, waits for them, and re-layouts  7.34 us (7%)
  matrix products  6.38 us (6%)
  other arithmetic  5.66 us (5%)
    unnamed x1, blocking collectives  41.9 us
    all_gather x1, blocking collectives, shards(): lax.all_gather(text_values, 'tile', axis=0, tiled=True)  21.4 us
    all_gather x1, blocking collectives, shards(): lax.all_gather(text_keys, 'tile', axis=0, tiled=True)  19.6 us
    ppermute x2, starting transfers between devices, passed_along(): lax.ppermute(value, axis, [(source, source + steps) for source in range(f...  7.75 us
    unnamed x15, local copies, waits for them, and re-layouts  4.48 us
    dot_general x4, matrix products, fold_block(): jnp.einsum('hqk,khd->hqd', weights, value_heads, preferred_element_type=j...  3.48 us
    reduce_sum x4, other arithmetic, fold_block(): row_total = row_total * scale_down + jnp.sum(exp_terms, axis=-1)  2.97 us
    dot_general x4, matrix products, fold_block(): jnp.einsum('qhd,khd->hqk', query_heads, key_heads, preferred_element_type...  2.9 us
  transfers between devices with their start and end apart: 2, of which 0 were waited for; matrix products, arithmetic and copies ran while one was open for 5% of the time, Pallas kernels for 0%

commit v1 on v0

--- a/solution.py
+++ b/solution.py
@@ -8,6 +8,18 @@
 HEAD_DIM = 128
 HEAD_GROUPS = 4
 MASKED = -1e30
+
+
+def collect(x, axis, dim):
+    ways, here, lap = (lax.axis_size(axis), lax.axis_index(axis), x.shape[dim])
+    line, have = (x, 1)
+    while have < ways:
+        line = jnp.concatenate(
+            [line, lax.ppermute(line, axis, [(d, (d - have) % ways) for d in range(ways)])],
+            axis=dim,
+        )
+        have = 2 * have
+    return jnp.roll(line, here * lap, axis=dim)
 
 
 def passed_along(value, axis, steps):
@@ -77,10 +89,7 @@
     )
     text_flags = text_mask.astype(jnp.bfloat16)
     piece_keys = lax.dynamic_slice_in_dim(
-        lax.all_gather(text_keys, "tile", axis=0, tiled=True),
-        head_group * lane_width,
-        lane_width,
-        1,
+        collect(text_keys, "tile", 0), head_group * lane_width, lane_width, 1
     )
     piece_values = lax.dynamic_slice_in_dim(
         lax.all_gather(text_values, "tile", axis=0, tiled=True),

time: 111 us -> 143 us (1.29)
  waiting for transfers between devices: 0.01 us -> 36.4 us
  blocking collectives: 82.9 us -> 64.6 us
  local copies, waits for them, and re-layouts: 7.34 us -> 13.3 us
  starting transfers between devices: 7.75 us -> 12 us
  other arithmetic: 5.66 us -> 7.93 us
    ppermute x0 -> x4, waiting for transfers between devices: none -> 36.4 us  [collect(): lax.ppermute(line, axis, [(d, (d - have) % ways) for d in range(ways)])]
    all_gather x1 -> x0, blocking collectives: 19.6 us -> none  [shards(): lax.all_gather(text_keys, 'tile', axis=0, tiled=True)]
    all_gather x1, blocking collectives: 21.4 us -> 34.8 us  [shards(): lax.all_gather(text_values, 'tile', axis=0, tiled=True)]
    unnamed x1, blocking collectives: 41.9 us -> 29.8 us
    concatenate x0 -> x1, local copies, waits for them, and re-layouts: none -> 5.62 us  [collect(): return jnp.roll(line, here * lap, axis=dim)]
    ppermute x0 -> x4, starting transfers between devices: none -> 4.93 us  [collect(): lax.ppermute(line, axis, [(d, (d - have) % ways) for d in range(ways)])]
    unnamed x15 -> x43, local copies, waits for them, and re-layouts: 4.48 us -> 4.73 us
  transfers between devices with their start and end apart: 2 -> 6, of which waited for: 0 -> 3; matrix products, arithmetic and copies ran while one was open for 5% -> 9% of each run, Pallas kernels for 0% -> 0%
where the time goes in v1:
time: 143 us
  blocking collectives  64.6 us (45%)
  waiting for transfers between devices  36.4 us (25%)
  local copies, waits for them, and re-layouts  13.3 us (9%)
  starting transfers between devices  12 us (8%)
  other arithmetic  7.93 us (6%)
  matrix products  7.36 us (5%)
    ppermute x4, waiting for transfers between devices, collect(): lax.ppermute(line, axis, [(d, (d - have) % ways) for d in range(ways)])  36.4 us
    all_gather x1, blocking collectives, shards(): lax.all_gather(text_values, 'tile', axis=0, tiled=True)  34.8 us
    unnamed x1, blocking collectives  29.8 us
    ppermute x2, starting transfers between devices, passed_along(): lax.ppermute(value, axis, [(source, source + steps) for source in range(f...  7.11 us
    concatenate x1, local copies, waits for them, and re-layouts, collect(): return jnp.roll(line, here * lap, axis=dim)  5.62 us
    ppermute x4, starting transfers between devices, collect(): lax.ppermute(line, axis, [(d, (d - have) % ways) for d in range(ways)])  4.93 us
    unnamed x43, local copies, waits for them, and re-layouts  4.73 us
    dot_general x4, matrix products, fold_block(): jnp.einsum('qhd,khd->hqk', query_heads, key_heads, preferred_element_type...  3.89 us
  transfers between devices with their start and end apart: 6, of which 3 were waited for; matrix products, arithmetic and copies ran while one was open for 9% of the time, Pallas kernels for 0%

profile of v1, /device:TPU:0, one launch (start us, length us, event | category | flops | bytes accessed | tf_op | source)
XLA Modules:
  0.0 142.7 jit_solution(7738860658897163337)
XLA Ops:
  0.0 1.2 copy.89
  1.3 1.3 copy.94
  2.6 1.3 fusion.71
  3.9 5.8 %collective-permute-start.4 = (bf16[2,512,384]{1,2,0:T(8,128)(2,1)}, bf16[2,512,384]{1,2,0:T(8,128)(2,1)}, u32[]{:S(2)}, u32[]{:S(2)}) collective-permute-start(bf16[2,512,384]{1,2,0:T(8,128)(2,1)} %get-tuple-element.16), channel_id=1, source_target_pairs={{0,4},{1,5},{2,6},{3,7},{4,8},{5,9},{6,10},{7,11},{8,12},{9,13},{1... | collective-permute-start | bytes 2359304 | tf_op jit(solution)/shard_map/ppermute | solution.py:28
  9.7 1.3 collective-permute-start.5
  11.2 4.6 %collective-permute-start = (bf16[16,1536]{0,1:T(8,128)(2,1)S(1)}, bf16[16,1536]{0,1:T(8,128)(2,1)S(1)}, u32[]{:S(2)}, u32[]{:S(2)}) collective-permute-start(bf16[16,1536]{0,1:T(8,128)(2,1)S(1)} %copy.82), channel_id=1, source_target_pairs={{0,15},{1,0},{2,1},{3,2},{4,3},{5,4},{6,5},{7,6},{8,7},{9,8},{10,9... | collective-permute-start | bytes 147464 | tf_op jit(solution)/shard_map/ppermute | solution.py:18
  15.8 34.8 %all_gather.7 = bf16[256,1536]{1,0:T(8,128)(2,1)S(1)} all-gather(bf16[16,1536]{1,0:T(8,128)(2,1)S(1)} %copy-done.12), channel_id=1, replica_groups=mesh['req'=2,'tile'=16] {'tile'}, dimensions={0}, use_global_device_ids=true | all-gather | bytes 835584 | tf_op jit(solution)/shard_map/all_gather | solution.py:95
  50.7 0.9 copy.84
  51.7 0.8 copy.87
  52.5 0.6 dynamic-slice
  54.0 29.8 %all-reduce = bf16[256]{0:T(256)(128)(2,1)S(1)} all-reduce(bf16[256]{0:T(256)(128)(2,1)S(1)} %dynamic-update-slice), channel_id=1, replica_groups=mesh['req'=2,'tile'=16] {'tile'}, use_global_device_ids=true, to_apply=%add | all-reduce | flops 256 | bytes 1024
  84.2 10.5 %collective-permute-done.1 = bf16[32,1536]{0,1:T(8,128)(2,1)S(1)} collective-permute-done((bf16[32,1536]{0,1:T(8,128)(2,1)S(1)}, bf16[32,1536]{0,1:T(8,128)(2,1)S(1)}, u32[]{:S(2)}, u32[]{:S(2)}) %collective-permute-start.1) | collective-permute-done | bytes 98336 | tf_op jit(solution)/shard_map/ppermute | solution.py:18
  94.7 0.4 pad_maximum_fusion.2
  95.3 0.6 broadcast_compare_fusion
  95.9 9.0 %collective-permute-done.2 = bf16[64,1536]{0,1:T(8,128)(2,1)S(1)} collective-permute-done((bf16[64,1536]{0,1:T(8,128)(2,1)S(1)}, bf16[64,1536]{0,1:T(8,128)(2,1)S(1)}, u32[]{:S(2)}, u32[]{:S(2)}) %collective-permute-start.2) | collective-permute-done | bytes 196640 | tf_op jit(solution)/shard_map/ppermute | solution.py:18
  104.9 0.5 pad_maximum_fusion.3
  105.7 0.8 fusion.4
  106.5 16.9 %collective-permute-done.3 = bf16[128,1536]{0,1:T(8,128)(2,1)} collective-permute-done((bf16[128,1536]{0,1:T(8,128)(2,1)S(1)}, bf16[128,1536]{0,1:T(8,128)(2,1)}, u32[]{:S(2)}, u32[]{:S(2)}) %collective-permute-start.3) | collective-permute-done | bytes 393248 | tf_op jit(solution)/shard_map/ppermute | solution.py:18
  123.4 5.6 %concatenate.21 = bf16[512,1536]{0,1:T(8,128)(2,1)} concatenate(bf16[16,1536]{0,1:T(8,128)(2,1)S(1)} %copy.82, bf16[16,1536]{0,1:T(8,128)(2,1)} %copy-done.2, bf16[32,1536]{0,1:T(8,128)(2,1)} %copy-done.3, bf16[64,1536]{0,1:T(8,128)(2,1)} %copy-done.6, bf16[128,1536]{0,1:T(8,128)(2,1)} %collective-permute-done.3, bf16[16,1536]{0,1:T(8,128)(2,1)S(1)} %copy.82, ...), dimensions={0} | concatenate | bytes 3145728 | tf_op jit(solution)/shard_map/jit(_roll_dynamic)/concatenate | solution.py:22
  129.0 1.1 dynamic_slice.8
  130.1 1.4 %bitcast_reduce_fusion.2 = (f32[3,512]{1,0:T(4,128)S(1)}, f32[3,256,512]{2,1,0:T(8,128)S(1)}) fusion(bf16[256,3,128]{0,2,1:T(8,128)(2,1)S(1)} %bitcast.168, bf16[512,3,128]{0,2,1:T(8,128)(2,1)} %bitcast.160, pred[256]{0:T(512)(128)(4,1)} %broadcast_compare_fusion), kind=kOutput, calls=%fused_computation.21 | convolution fusion | flops 101841408 | bytes 2169088 | tf_op jit(solution)/shard_map/qhd,khd->hqk/dot_general | solution.py:40
  131.5 1.9 %maximum_bitcast_fusion = bf16[1,3,2,512,384]{3,4,2,1,0:T(8,128)(2,1)S(1)} fusion(bf16[1,2,512,384]{2,3,1,0:T(8,128)(2,1)} %bitcast.13, bf16[1,2,512,384]{2,3,1,0:T(8,128)(2,1)} %get-tuple-element.15, bf16[1,2,512,384]{2,3,1,0:T(8,128)(2,1)} %bitcast.11), kind=kLoop, calls=%fused_computation.13 | loop fusion | flops 2359296 | bytes 4718592 | tf_op jit(solution)/shard_map/stack | solution.py:120
  133.6 0.8 bitcast_reduce_fusion.1
  134.4 0.8 bitcast_reduce_fusion
  135.3 0.9 fusion.5
  136.2 1.0 fusion.24
  137.1 0.9 fusion.7
  138.0 1.0 fusion.35
  139.0 0.9 fusion.9
  139.9 1.0 fusion.38
  141.2 0.6 fusion.43
  141.8 0.9 copy.104
  (54 shorter events, 1.8 us)
Async XLA Ops:
  0.0 11.0 %copy-start.11 = (bf16[16,1536]{1,0:T(8,128)(2,1)S(1)}, bf16[16,1536]{1,0:T(8,128)(2,1)}, u32[]{:S(2)}) copy-start(bf16[16,1536]{1,0:T(8,128)(2,1)} %param.9) | copy-start | bytes 147460
  0.0 15.8 %copy-start.12 = (bf16[16,1536]{1,0:T(8,128)(2,1)S(1)}, bf16[16,1536]{1,0:T(8,128)(2,1)}, u32[]{:S(2)}) copy-start(bf16[16,1536]{1,0:T(8,128)(2,1)} %param.10) | copy-start | bytes 147460
  0.0 50.7 %copy-start.9 = (bf16[1,512,384]{2,1,0:T(8,128)(2,1)S(1)}, bf16[1,512,384]{2,1,0:T(8,128)(2,1)}, u32[]{:S(2)}) copy-start(bf16[1,512,384]{2,1,0:T(8,128)(2,1)} %param.6) | copy-start | bytes 1179652
  0.0 51.6 %copy-start.16 = (s32[16]{0:T(128)S(1)}, s32[16]{0:T(128)}, u32[]{:S(2)}) copy-start(s32[16]{0:T(128)} %param.11) | copy-start | bytes 196
  1.2 82.9 %copy-start.4 = (bf16[1,512,384]{1,2,0:T(8,128)(2,1)}, bf16[1,512,384]{1,2,0:T(8,128)(2,1)S(1)}, u32[]{:S(2)}) copy-start(bf16[1,512,384]{1,2,0:T(8,128)(2,1)S(1)} %copy.89) | copy-start | bytes 1179652
  1.2 51.2 %copy-start.17 = (u32[32]{0:T(128)S(1)}, u32[32]{0:T(128)}, u32[]{:S(2)}) copy-start(u32[32]{0:T(128)} %constant.138) | copy-start | bytes 388
  2.6 7.1 %copy-start.7 = (bf16[1,512,384]{1,2,0:T(8,128)(2,1)}, bf16[1,512,384]{1,2,0:T(8,128)(2,1)S(1)}, u32[]{:S(2)}) copy-start(bf16[1,512,384]{1,2,0:T(8,128)(2,1)S(1)} %copy.94) | copy-start | bytes 1179652
  3.9 127.6 %collective-permute-start.4 = (bf16[2,512,384]{1,2,0:T(8,128)(2,1)}, bf16[2,512,384]{1,2,0:T(8,128)(2,1)}, u32[]{:S(2)}, u32[]{:S(2)}) collective-permute-start(bf16[2,512,384]{1,2,0:T(8,128)(2,1)} %get-tuple-element.16), channel_id=1, source_target_pairs={{0,4},{1,5},{2,6},{3,7},{4,8},{5,9},{6,10},{7,11},{8,12},{9,13},{1... | collective-permute-start | bytes 2359304 | tf_op jit(solution)/shard_map/ppermute | solution.py:28
  9.7 121.8 %collective-permute-start.5 = (bf16[2,512,384]{1,2,0:T(8,128)(2,1)}, bf16[2,512,384]{1,2,0:T(8,128)(2,1)}, u32[]{:S(2)}, u32[]{:S(2)}) collective-permute-start(bf16[2,512,384]{1,2,0:T(8,128)(2,1)} %get-tuple-element.16), channel_id=1, source_target_pairs={{4,0},{5,1},{6,2},{7,3},{8,4},{9,5},{10,6},{11,7},{12,8},{13,9},{1... | collective-permute-start | bytes 2359304 | tf_op jit(solution)/shard_map/ppermute | solution.py:28
  11.2 72.6 %collective-permute-start = (bf16[16,1536]{0,1:T(8,128)(2,1)S(1)}, bf16[16,1536]{0,1:T(8,128)(2,1)S(1)}, u32[]{:S(2)}, u32[]{:S(2)}) collective-permute-start(bf16[16,1536]{0,1:T(8,128)(2,1)S(1)} %copy.82), channel_id=1, source_target_pairs={{0,15},{1,0},{2,1},{3,2},{4,3},{5,4},{6,5},{7,6},{8,7},{9,8},{10,9... | collective-permute-start | bytes 147464 | tf_op jit(solution)/shard_map/ppermute | solution.py:18
  83.8 21.8 %copy-start = (bf16[1,512,384]{1,2,0:T(8,128)(2,1)S(1)}, bf16[1,512,384]{1,2,0:T(8,128)(2,1)}, u32[]{:S(2)}) copy-start(bf16[1,512,384]{1,2,0:T(8,128)(2,1)} %copy.84) | copy-start | bytes 1179652
  83.8 21.7 %copy-start.2 = (bf16[16,1536]{0,1:T(8,128)(2,1)}, bf16[16,1536]{0,1:T(8,128)(2,1)S(1)}, u32[]{:S(2)}) copy-start(bf16[16,1536]{0,1:T(8,128)(2,1)S(1)} %collective-permute-done) | copy-start | bytes 147460
  84.1 10.6 %collective-permute-start.1 = (bf16[32,1536]{0,1:T(8,128)(2,1)S(1)}, bf16[32,1536]{0,1:T(8,128)(2,1)S(1)}, u32[]{:S(2)}, u32[]{:S(2)}) collective-permute-start(bf16[32,1536]{0,1:T(8,128)(2,1)S(1)} %pad_maximum_fusion.1), channel_id=1, source_target_pairs={{0,14},{1,15},{2,0},{3,1},{4,2},{5,3},{6,4},{7,5},{8,6},{9,7},{10,... | collective-permute-start | bytes 294920 | tf_op jit(solution)/shard_map/ppermute | solution.py:18
  84.2 21.5 %copy-start.5 = (bf16[1,512,384]{1,2,0:T(8,128)(2,1)S(1)}, bf16[1,512,384]{1,2,0:T(8,128)(2,1)}, u32[]{:S(2)}) copy-start(bf16[1,512,384]{1,2,0:T(8,128)(2,1)} %copy-done.4) | copy-start | bytes 1179652
  94.7 10.9 %copy-start.3 = (bf16[32,1536]{0,1:T(8,128)(2,1)}, bf16[32,1536]{0,1:T(8,128)(2,1)S(1)}, u32[]{:S(2)}) copy-start(bf16[32,1536]{0,1:T(8,128)(2,1)S(1)} %collective-permute-done.1) | copy-start | bytes 294916
  95.1 9.9 %collective-permute-start.2 = (bf16[64,1536]{0,1:T(8,128)(2,1)S(1)}, bf16[64,1536]{0,1:T(8,128)(2,1)S(1)}, u32[]{:S(2)}, u32[]{:S(2)}) collective-permute-start(bf16[64,1536]{0,1:T(8,128)(2,1)S(1)} %pad_maximum_fusion.2), channel_id=1, source_target_pairs={{0,12},{1,13},{2,14},{3,15},{4,0},{5,1},{6,2},{7,3},{8,4},{9,5},{1... | collective-permute-start | bytes 589832 | tf_op jit(solution)/shard_map/ppermute | solution.py:18
  104.9 0.8 copy-start.6
  105.4 17.9 %collective-permute-start.3 = (bf16[128,1536]{0,1:T(8,128)(2,1)S(1)}, bf16[128,1536]{0,1:T(8,128)(2,1)}, u32[]{:S(2)}, u32[]{:S(2)}) collective-permute-start(bf16[128,1536]{0,1:T(8,128)(2,1)S(1)} %pad_maximum_fusion.3), channel_id=1, source_target_pairs={{0,8},{1,9},{2,10},{3,11},{4,12},{5,13},{6,14},{7,15},{8,0},{9,1},... | collective-permute-start | bytes 1179656 | tf_op jit(solution)/shard_map/ppermute | solution.py:18
  105.5 1.0 copy-start.14
  131.5 2.0 %copy-start.1 = (bf16[1,512,384]{1,2,0:T(8,128)(2,1)S(1)}, bf16[1,512,384]{1,2,0:T(8,128)(2,1)}, u32[]{:S(2)}) copy-start(bf16[1,512,384]{1,2,0:T(8,128)(2,1)} %copy.84) | copy-start | bytes 1179652
  133.6 1.7 %copy-start.15 = (pred[512]{0:T(512)(128)(4,1)S(1)}, pred[512]{0:T(512)(128)(4,1)}, u32[]{:S(2)}) copy-start(pred[512]{0:T(512)(128)(4,1)} %copy-done.14) | copy-start | bytes 1540
  134.4 1.8 %copy-start.8 = (bf16[1,512,384]{1,2,0:T(8,128)(2,1)S(1)}, bf16[1,512,384]{1,2,0:T(8,128)(2,1)}, u32[]{:S(2)}) copy-start(bf16[1,512,384]{1,2,0:T(8,128)(2,1)} %copy-done.7) | copy-start | bytes 1179652
  139.9 1.0 copy-start.13
  139.9 1.4 copy-start.10
